TPU v7x, 32 devices: a whole 2x2x4 slice. The times are simulated.
32 devices in a mesh: groups: 2 (over y), seq: 4 (over z), chan: 4 (over x, core).
Axes of the slice: x: 2, y: 2, z: 4, core: 2. Of those that a mesh axis runs over, the one named last changes fastest.
Arguments:
- value: bfloat16 [1024, 4096], P(('groups', 'seq'), 'chan'), parts along dimension 0, may hold values from -6 to 6
- first_gate: bfloat16 [1024, 4096], P(('groups', 'seq'), 'chan'), parts along dimension 0, may hold values from -6 to 6
- second_gate: bfloat16 [1024, 4096], P(('groups', 'seq'), 'chan'), parts along dimension 0, may hold values from -6 to 6
- first_filter: bfloat16 [256, 512], P('chan'), may hold values from -0.25 to 0.25
- second_filter: bfloat16 [256, 512], P('chan'), may hold values from -0.25 to 0.25
- out_weight: bfloat16 [4096, 4096], P('chan'), may hold values from -0.09375 to 0.09375
- segment_ids: int32 [1024], P(('groups', 'seq')), parts along dimension 0, may hold values from 0 to 1, never falling along the last dimension, each value on 1 to 384 neighbouring positions
Outputs:
- mixed: bfloat16 [1024, 4096], P(('groups', 'seq')), parts along dimension 0
There are 2 independent parts, one for each index of `groups`. A program takes and returns all parts, laid end to end along the dimension named above; an argument that names none is the same for every part. Nothing has to cross between parts.
Inputs may be any that keep to these rules, and one draw needn't show every extreme that they name: `segment_ids`: ids never fall along the window; the 2 contexts each hold 128 to 384 neighbouring positions and together fill the window.
All inputs are finite; a program needn't handle non-finite values.
Results may differ from a plain program's by a relative error of at most 0.0065.
Values may be sent and summed in bfloat16 or wider, within the bound.
No kernel may reach another device: no remote copies, remote signals or barrier semaphores. Data moves between devices by JAX's collectives and lax.ppermute only.
A program may use at most 192 MiB of HBM per device.

v0:
```python
import jax
import jax.numpy as jnp
from jax import lax
from jax.sharding import PartitionSpec as P


def toeplitz_taps(doubled, length, base, rows, cols, row_segs, col_segs):
    filt_count = doubled.shape[0]
    span = rows + cols
    start = jnp.mod(base - cols + 1, length)
    window = lax.dynamic_slice_in_dim(doubled, start, span - 1, 1)
    reversed_win = jnp.concatenate(
        [window[:, ::-1], jnp.zeros((filt_count, 1), doubled.dtype)], axis=1
    )
    tiled = jnp.tile(reversed_win, (1, rows))[:, : rows * (span - 1)]
    skewed = tiled.reshape(filt_count, rows, span - 1)[:, :, rows - 1 : rows - 1 + cols]
    same = (row_segs[:, None] == col_segs[None, :]).astype(doubled.dtype)
    return skewed * same[None, :, :]


def apply_taps(grouped, taps):
    return jnp.einsum("gcs,gts->gct", grouped, taps, preferred_element_type=jnp.float32)


def to_rows(result):
    filt_count, per_filter, rows = result.shape
    return result.transpose(2, 0, 1).reshape(rows, filt_count * per_filter)


def local(value, first_gate, second_gate, first_filter, second_filter, out_weight, segment_ids):
    tok_rows = value.shape[0]
    chans = value.shape[1]
    filt_count = first_filter.shape[0]
    length = first_filter.shape[1]
    per_filter = chans // filt_count
    my_start = lax.axis_index("seq") * tok_rows
    seg_row = segment_ids.reshape(1, tok_rows)

    def long_conv(filters, field):
        doubled = jnp.concatenate([filters, filters], axis=1)
        field_cols = field.T
        empty = jnp.zeros((filt_count, per_filter, tok_rows), jnp.float32)
        piece_field = lax.all_gather(field_cols, "seq", axis=1, tiled=True)
        piece_segs = lax.all_gather(seg_row, "seq", axis=1, tiled=True)
        cols = piece_field.shape[1]
        steps_count = cols // tok_rows

        def one_block(index, acc):
            offset = (index * tok_rows).astype(jnp.int32)
            sub_field = lax.dynamic_slice_in_dim(piece_field, offset, tok_rows, 1)
            sub_segs = lax.dynamic_slice_in_dim(piece_segs[0], offset, tok_rows, 0)
            grouped = sub_field.reshape(filt_count, per_filter, tok_rows)
            taps = toeplitz_taps(
                doubled, length, my_start - offset, tok_rows, tok_rows, segment_ids, sub_segs
            )
            return acc + apply_taps(grouped, taps)

        total = lax.fori_loop(0, steps_count, one_block, empty)
        return to_rows(total)

    first_input = (first_gate.astype(jnp.float32) * value.astype(jnp.float32)).astype(jnp.bfloat16)
    first_mix = long_conv(first_filter, first_input)
    second_input = (second_gate.astype(jnp.float32) * first_mix).astype(jnp.bfloat16)
    second_mix = long_conv(second_filter, second_input).astype(jnp.bfloat16)
    partial_out = jnp.dot(second_mix, out_weight, preferred_element_type=jnp.float32)
    mixed = lax.psum(partial_out, "chan").astype(jnp.bfloat16)
    return mixed


def solution(mesh):
    in_specs = (
        P(("groups", "seq"), "chan"),
        P(("groups", "seq"), "chan"),
        P(("groups", "seq"), "chan"),
        P("chan", None),
        P("chan", None),
        P("chan", None),
        P(("groups", "seq")),
    )
    out_specs = P(("groups", "seq"), None)
    return jax.shard_map(local, mesh=mesh, in_specs=in_specs, out_specs=out_specs, check_vma=False)
```

profile of v0, /device:TPU:0, one launch (start us, length us, event | category | flops | bytes accessed | tf_op | source)
XLA Modules:
  0.0 331.7 jit_solution(859946293358869970)
XLA Ops:
  6.5 1.1 copy.15
  7.7 1.1 copy.16
  8.8 0.8 fusion.9
  9.7 1.1 copy.14
  10.8 12.8 %all-gather.1 = s32[4,1,128]{2,1,0:T(1,128)S(1)} all-gather(s32[1,1,128]{2,1,0:T(1,128)} %bitcast.64), channel_id=2, replica_groups=mesh['groups'=2,'seq'=4,'chan'=4] {'seq'}, dimensions={0}, use_global_device_ids=true | all-gather | bytes 2560 | tf_op jit(solution)/shard_map/all_gather | solution.py:44
  23.6 0.9 pad_maximum_fusion
  24.5 17.9 %all-gather.5.cloned.1.call-done = bf16[1024,512]{1,0:T(8,128)(2,1)} async-done(((bf16[1024,128]{1,0:T(8,128)(2,1)}), bf16[1024,512]{1,0:T(8,128)(2,1)}) %all-gather.5.cloned.1.call-update) | async-done | bytes 1048592 | tf_op jit(solution)/shard_map/all_gather | solution.py:43
  42.4 103.7 %while.36 = (s32[]{:T(128)}, f32[64,16,128]{2,1,0:T(8,128)S(1)}, bf16[1024,512]{1,0:T(8,128)(2,1)}, s32[]{:T(128)}, bf16[64,1024]{1,0:T(8,128)(2,1)S(1)}, /*inde...) while((s32[]{:T(128)}, f32[64,16,128]{2,1,0:T(8,128)S(1)}, ...), condition=%wide.region_1.2_spmd.clone, body=%wide.region_0.1_spmd.clone.sunk | while | flops 34897944 | bytes 33591060 | solution.py:58
  42.8 0.3 tile.60
  43.1 2.6 copy.21
  45.7 2.3 slice.78
  47.9 15.8 %reshape.158 = bf16[64,128,255]{2,1,0:T(8,128)(2,1)} reshape(bf16[64,32640]{1,0:T(8,128)(2,1)} %slice.78) | data formatting | bytes 8355840 | tf_op jit(solution)/shard_map/while/body/eval_jaxpr/reshape | solution.py:16
  63.9 1.0 constant_dynamic-slice_fusion.10
  64.8 3.5 %fusion.23 = f32[64,16,128]{2,1,0:T(8,128)S(1)} fusion(bf16[64,16,128]{2,1,0:T(8,128)(2,1)S(1)} %bitcast.58, bf16[64,128,255]{2,1,0:T(8,128)(2,1)} %reshape.158, bf16[128,128]{1,0:T(8,128)(2,1)S(1)} %compare_convert_fusion.4, f32[64,16,128]{2,1,0:T(8,128)S(1)} %get-tuple-element.645, pred[]{:T(512)S(6)} %compare.16), kind=kOutput, calls=%fused_computation.2.clone.1 | convolution fusion | flops 34865152 | bytes 3440641 | tf_op jit(solution)/shard_map/while/body/eval_jaxpr/gcs,gts->gct/dot_general | solution.py:22
  68.7 0.3 tile.60
  69.0 2.6 copy.21
  71.6 2.3 slice.78
  73.9 15.8 %reshape.158 = bf16[64,128,255]{2,1,0:T(8,128)(2,1)} reshape(bf16[64,32640]{1,0:T(8,128)(2,1)} %slice.78) | data formatting | bytes 8355840 | tf_op jit(solution)/shard_map/while/body/eval_jaxpr/reshape | solution.py:16
  89.8 1.0 constant_dynamic-slice_fusion.10
  90.8 3.5 %fusion.23 = f32[64,16,128]{2,1,0:T(8,128)S(1)} fusion(bf16[64,16,128]{2,1,0:T(8,128)(2,1)S(1)} %bitcast.58, bf16[64,128,255]{2,1,0:T(8,128)(2,1)} %reshape.158, bf16[128,128]{1,0:T(8,128)(2,1)S(1)} %compare_convert_fusion.4, f32[64,16,128]{2,1,0:T(8,128)S(1)} %get-tuple-element.645, pred[]{:T(512)S(6)} %compare.16), kind=kOutput, calls=%fused_computation.2.clone.1 | convolution fusion | flops 34865152 | bytes 3440641 | tf_op jit(solution)/shard_map/while/body/eval_jaxpr/gcs,gts->gct/dot_general | solution.py:22
  94.4 0.2 reverse.4
  94.6 0.3 tile.60
  94.9 2.6 copy.21
  97.5 2.3 slice.78
  99.8 15.8 %reshape.158 = bf16[64,128,255]{2,1,0:T(8,128)(2,1)} reshape(bf16[64,32640]{1,0:T(8,128)(2,1)} %slice.78) | data formatting | bytes 8355840 | tf_op jit(solution)/shard_map/while/body/eval_jaxpr/reshape | solution.py:16
  115.7 1.0 constant_dynamic-slice_fusion.10
  116.7 3.5 %fusion.23 = f32[64,16,128]{2,1,0:T(8,128)S(1)} fusion(bf16[64,16,128]{2,1,0:T(8,128)(2,1)S(1)} %bitcast.58, bf16[64,128,255]{2,1,0:T(8,128)(2,1)} %reshape.158, bf16[128,128]{1,0:T(8,128)(2,1)S(1)} %compare_convert_fusion.4, f32[64,16,128]{2,1,0:T(8,128)S(1)} %get-tuple-element.645, pred[]{:T(512)S(6)} %compare.16), kind=kOutput, calls=%fused_computation.2.clone.1 | convolution fusion | flops 34865152 | bytes 3440641 | tf_op jit(solution)/shard_map/while/body/eval_jaxpr/gcs,gts->gct/dot_general | solution.py:22
  120.3 0.2 reverse.4
  120.6 0.3 tile.60
  120.9 2.6 copy.21
  123.5 2.3 slice.78
  125.7 15.8 %reshape.158 = bf16[64,128,255]{2,1,0:T(8,128)(2,1)} reshape(bf16[64,32640]{1,0:T(8,128)(2,1)} %slice.78) | data formatting | bytes 8355840 | tf_op jit(solution)/shard_map/while/body/eval_jaxpr/reshape | solution.py:16
  141.7 1.0 constant_dynamic-slice_fusion.10
  142.7 3.5 %fusion.23 = f32[64,16,128]{2,1,0:T(8,128)S(1)} fusion(bf16[64,16,128]{2,1,0:T(8,128)(2,1)S(1)} %bitcast.58, bf16[64,128,255]{2,1,0:T(8,128)(2,1)} %reshape.158, bf16[128,128]{1,0:T(8,128)(2,1)S(1)} %compare_convert_fusion.4, f32[64,16,128]{2,1,0:T(8,128)S(1)} %get-tuple-element.645, pred[]{:T(512)S(6)} %compare.16), kind=kOutput, calls=%fused_computation.2.clone.1 | convolution fusion | flops 34865152 | bytes 3440641 | tf_op jit(solution)/shard_map/while/body/eval_jaxpr/gcs,gts->gct/dot_general | solution.py:22
  146.1 0.8 fusion.8
  146.9 28.3 %all-gather.7.cloned.1.call-done = bf16[1024,512]{1,0:T(8,128)(2,1)} async-done(((bf16[1024,128]{1,0:T(8,128)(2,1)}), bf16[1024,512]{1,0:T(8,128)(2,1)}) %all-gather.7.cloned.1.call-update) | async-done | bytes 1048592 | tf_op jit(solution)/shard_map/all_gather | solution.py:43
  175.3 103.7 %while.37 = (s32[]{:T(128)}, f32[64,16,128]{2,1,0:T(8,128)S(1)}, bf16[1024,512]{1,0:T(8,128)(2,1)}, s32[]{:T(128)}, bf16[64,1024]{1,0:T(8,128)(2,1)S(1)}, /*inde...) while((s32[]{:T(128)}, f32[64,16,128]{2,1,0:T(8,128)S(1)}, ...), condition=%wide.region_3.4_spmd.clone, body=%wide.region_2.3_spmd.clone.sunk | while | flops 34897944 | bytes 33591060 | solution.py:58
  175.7 0.3 tile.61
  175.9 2.6 copy.22
  178.6 2.3 slice.81
  180.8 15.8 %reshape.159 = bf16[64,128,255]{2,1,0:T(8,128)(2,1)} reshape(bf16[64,32640]{1,0:T(8,128)(2,1)} %slice.81) | data formatting | bytes 8355840 | tf_op jit(solution)/shard_map/while/body/eval_jaxpr/reshape | solution.py:16
  196.8 1.0 constant_dynamic-slice_fusion.12
  197.7 3.5 %fusion.26 = f32[64,16,128]{2,1,0:T(8,128)S(1)} fusion(bf16[64,16,128]{2,1,0:T(8,128)(2,1)S(1)} %bitcast.59, bf16[64,128,255]{2,1,0:T(8,128)(2,1)} %reshape.159, bf16[128,128]{1,0:T(8,128)(2,1)S(1)} %compare_convert_fusion.5, f32[64,16,128]{2,1,0:T(8,128)S(1)} %get-tuple-element.690, pred[]{:T(512)S(6)} %compare.17), kind=kOutput, calls=%fused_computation.11.clone.1 | convolution fusion | flops 34865152 | bytes 3440641 | tf_op jit(solution)/shard_map/while/body/eval_jaxpr/gcs,gts->gct/dot_general | solution.py:22
  201.3 0.2 reverse.5
  201.6 0.3 tile.61
  201.9 2.6 copy.22
  204.5 2.3 slice.81
  206.7 15.8 %reshape.159 = bf16[64,128,255]{2,1,0:T(8,128)(2,1)} reshape(bf16[64,32640]{1,0:T(8,128)(2,1)} %slice.81) | data formatting | bytes 8355840 | tf_op jit(solution)/shard_map/while/body/eval_jaxpr/reshape | solution.py:16
  222.7 1.0 constant_dynamic-slice_fusion.12
  223.7 3.5 %fusion.26 = f32[64,16,128]{2,1,0:T(8,128)S(1)} fusion(bf16[64,16,128]{2,1,0:T(8,128)(2,1)S(1)} %bitcast.59, bf16[64,128,255]{2,1,0:T(8,128)(2,1)} %reshape.159, bf16[128,128]{1,0:T(8,128)(2,1)S(1)} %compare_convert_fusion.5, f32[64,16,128]{2,1,0:T(8,128)S(1)} %get-tuple-element.690, pred[]{:T(512)S(6)} %compare.17), kind=kOutput, calls=%fused_computation.11.clone.1 | convolution fusion | flops 34865152 | bytes 3440641 | tf_op jit(solution)/shard_map/while/body/eval_jaxpr/gcs,gts->gct/dot_general | solution.py:22
  227.5 0.3 tile.61
  227.8 2.6 copy.22
  230.4 2.3 slice.81
  232.7 15.8 %reshape.159 = bf16[64,128,255]{2,1,0:T(8,128)(2,1)} reshape(bf16[64,32640]{1,0:T(8,128)(2,1)} %slice.81) | data formatting | bytes 8355840 | tf_op jit(solution)/shard_map/while/body/eval_jaxpr/reshape | solution.py:16
  248.6 1.0 constant_dynamic-slice_fusion.12
  249.6 3.5 %fusion.26 = f32[64,16,128]{2,1,0:T(8,128)S(1)} fusion(bf16[64,16,128]{2,1,0:T(8,128)(2,1)S(1)} %bitcast.59, bf16[64,128,255]{2,1,0:T(8,128)(2,1)} %reshape.159, bf16[128,128]{1,0:T(8,128)(2,1)S(1)} %compare_convert_fusion.5, f32[64,16,128]{2,1,0:T(8,128)S(1)} %get-tuple-element.690, pred[]{:T(512)S(6)} %compare.17), kind=kOutput, calls=%fused_computation.11.clone.1 | convolution fusion | flops 34865152 | bytes 3440641 | tf_op jit(solution)/shard_map/while/body/eval_jaxpr/gcs,gts->gct/dot_general | solution.py:22
  253.5 0.3 tile.61
  253.8 2.6 copy.22
  256.4 2.3 slice.81
  258.6 15.8 %reshape.159 = bf16[64,128,255]{2,1,0:T(8,128)(2,1)} reshape(bf16[64,32640]{1,0:T(8,128)(2,1)} %slice.81) | data formatting | bytes 8355840 | tf_op jit(solution)/shard_map/while/body/eval_jaxpr/reshape | solution.py:16
  274.6 1.0 constant_dynamic-slice_fusion.12
  275.5 3.5 %fusion.26 = f32[64,16,128]{2,1,0:T(8,128)S(1)} fusion(bf16[64,16,128]{2,1,0:T(8,128)(2,1)S(1)} %bitcast.59, bf16[64,128,255]{2,1,0:T(8,128)(2,1)} %reshape.159, bf16[128,128]{1,0:T(8,128)(2,1)S(1)} %compare_convert_fusion.5, f32[64,16,128]{2,1,0:T(8,128)S(1)} %get-tuple-element.690, pred[]{:T(512)S(6)} %compare.17), kind=kOutput, calls=%fused_computation.11.clone.1 | convolution fusion | flops 34865152 | bytes 3440641 | tf_op jit(solution)/shard_map/while/body/eval_jaxpr/gcs,gts->gct/dot_general | solution.py:22
  279.1 4.7 %fusion.10 = f32[128,4096]{1,0:T(8,128)S(1)} fusion(bf16[128,1024]{0,1:T(8,128)(2,1)S(1)} %bitcast.62, bf16[1024,4096]{1,0:T(8,128)(2,1)} %param.16), kind=kOutput, calls=%fused_computation.24 | convolution fusion | flops 1073741824 | bytes 10747904 | tf_op jit(solution)/shard_map/dot_general | solution.py:65
  283.7 41.1 %all-reduce.3 = bf16[128,4096]{1,0:T(8,128)(2,1)} all-reduce(f32[128,4096]{1,0:T(8,128)S(1)} %fusion.10), channel_id=1, replica_groups=mesh['groups'=2,'seq'=4,'chan'=4] {'chan'}, use_global_device_ids=true, to_apply=%region_4.5 | all-reduce | flops 524288 | bytes 3145728 | tf_op jit(solution)/shard_map/psum | solution.py:66
  (71 shorter events, 3.2 us)
Async XLA Ops:
  6.5 35.9 %all-gather.5.cloned.1.call-start = ((), (), s32[]{:S(2)}) async-start(), calls=%async_computation | async-start | bytes 1310720 | tf_op jit(solution)/shard_map/all_gather | solution.py:43
  9.6 165.7 %all-gather.7.cloned.1.call-start = ((), (), s32[]{:S(2)}) async-start(), calls=%async_computation.1 | async-start | bytes 1310720 | tf_op jit(solution)/shard_map/all_gather | solution.py:43
  42.4 104.5 %copy-start = (bf16[64,512]{1,0:T(8,128)(2,1)S(1)}, bf16[64,512]{1,0:T(8,128)(2,1)}, u32[]{:S(2)}) copy-start(bf16[64,512]{1,0:T(8,128)(2,1)} %param.15) | copy-start | bytes 196612
  47.9 15.8 %copy-start.1 = (s32[128]{0:T(128)S(1)}, s32[128]{0:T(128)}, u32[]{:S(2)}) copy-start(s32[128]{0:T(128)} %get-tuple-element.664) | copy-start | bytes 1540 | tf_op jit(solution)/shard_map/while
  73.9 15.8 %copy-start.1 = (s32[128]{0:T(128)S(1)}, s32[128]{0:T(128)}, u32[]{:S(2)}) copy-start(s32[128]{0:T(128)} %get-tuple-element.664) | copy-start | bytes 1540 | tf_op jit(solution)/shard_map/while
  99.8 15.8 %copy-start.1 = (s32[128]{0:T(128)S(1)}, s32[128]{0:T(128)}, u32[]{:S(2)}) copy-start(s32[128]{0:T(128)} %get-tuple-element.664) | copy-start | bytes 1540 | tf_op jit(solution)/shard_map/while
  125.7 15.8 %copy-start.1 = (s32[128]{0:T(128)S(1)}, s32[128]{0:T(128)}, u32[]{:S(2)}) copy-start(s32[128]{0:T(128)} %get-tuple-element.664) | copy-start | bytes 1540 | tf_op jit(solution)/shard_map/while
  180.8 15.8 %copy-start.2 = (s32[128]{0:T(128)S(1)}, s32[128]{0:T(128)}, u32[]{:S(2)}) copy-start(s32[128]{0:T(128)} %get-tuple-element.709) | copy-start | bytes 1540 | tf_op jit(solution)/shard_map/while
  206.7 15.8 %copy-start.2 = (s32[128]{0:T(128)S(1)}, s32[128]{0:T(128)}, u32[]{:S(2)}) copy-start(s32[128]{0:T(128)} %get-tuple-element.709) | copy-start | bytes 1540 | tf_op jit(solution)/shard_map/while
  232.7 15.8 %copy-start.2 = (s32[128]{0:T(128)S(1)}, s32[128]{0:T(128)}, u32[]{:S(2)}) copy-start(s32[128]{0:T(128)} %get-tuple-element.709) | copy-start | bytes 1540 | tf_op jit(solution)/shard_map/while
  258.6 15.8 %copy-start.2 = (s32[128]{0:T(128)S(1)}, s32[128]{0:T(128)}, u32[]{:S(2)}) copy-start(s32[128]{0:T(128)} %get-tuple-element.709) | copy-start | bytes 1540 | tf_op jit(solution)/shard_map/while
Sparse Core Ops, SparseCore 0:
  9.7 32.6 all-gather.4
  147.0 28.2 all-gather.6
where the time goes:
time: 333 us; the launch traced here: 332 us
  local copies, waits for them, and re-layouts  182 us (55%)
  blocking collectives  53.9 us (16%)
  waiting for transfers between devices  46.3 us (14%)
  matrix products  32.3 us (10%)
  between operations  13.5 us (4%)
    reshape x8, local copies, waits for them, and re-layouts, toeplitz_taps(): tiled.reshape(filt_count, rows, span - 1)[:, :, rows - 1:rows - 1 + cols]  127 us
    all_gather x2, waiting for transfers between devices, long_conv(): piece_field = lax.all_gather(field_cols, 'seq', axis=1, tiled=True)  46.2 us
    psum x1, blocking collectives, local(): mixed = lax.psum(partial_out, 'chan').astype(jnp.bfloat16)  41.1 us
    dot_general x8, matrix products, apply_taps(): jnp.einsum('gcs,gts->gct', grouped, taps, preferred_element_type=jnp.floa...  27.7 us
    while x40, local copies, waits for them, and re-layouts  23 us
    slice x8, local copies, waits for them, and re-layouts, toeplitz_taps(): tiled = jnp.tile(reversed_win, (1, rows))[:, :rows * (span - 1)]  18 us
    all_gather x1, blocking collectives, long_conv(): piece_segs = lax.all_gather(seg_row, 'seq', axis=1, tiled=True)  12.8 us
    dynamic_slice x8, local copies, waits for them, and re-layouts, one_block(): sub_field = lax.dynamic_slice_in_dim(piece_field, offset, tok_rows, 1)  7.8 us
  transfers between devices with their start and end apart: 2, of which 2 were waited for; matrix products, arithmetic and copies ran while one was open for 1% of the time, Pallas kernels for 0%

commit v1 on v0

--- a/solution.py
+++ b/solution.py
@@ -63,7 +63,7 @@
     second_input = (second_gate.astype(jnp.float32) * first_mix).astype(jnp.bfloat16)
     second_mix = long_conv(second_filter, second_input).astype(jnp.bfloat16)
     partial_out = jnp.dot(second_mix, out_weight, preferred_element_type=jnp.float32)
-    mixed = lax.psum(partial_out, "chan").astype(jnp.bfloat16)
+    mixed = jnp.sum(lax.all_gather(partial_out, "chan"), axis=0).astype(jnp.bfloat16)
     return mixed
 
 

time: 333 us -> 355 us (1.066)
  waiting for transfers between devices: 46.3 us -> 103 us
  blocking collectives: 53.9 us -> 12.8 us
  other arithmetic: 3.19 us -> 8.45 us
    all_gather x0 -> x1, waiting for transfers between devices: none -> 56.7 us  [local(): lax.all_gather(partial_out, 'chan')]
    psum x1 -> x0, blocking collectives: 41.1 us -> none  [local(): mixed = lax.psum(partial_out, 'chan').astype(jnp.bfloat16)]
    reduce_sum x0 -> x1, other arithmetic: none -> 5.26 us  [local(): jnp.sum(lax.all_gather(partial_out, 'chan'), axis=0).astype(jnp.bfloat16)]
  transfers between devices with their start and end apart: 2 -> 3, of which waited for: 2 -> 3; matrix products, arithmetic and copies ran while one was open for 1% -> 1% of each run, Pallas kernels for 0% -> 0%
where the time goes in v1:
time: 355 us; the launch traced here: 354 us
  local copies, waits for them, and re-layouts  182 us (51%)
  waiting for transfers between devices  103 us (29%)
  matrix products  33.7 us (9%)
  between operations  13.2 us (4%)
  blocking collectives  12.8 us (4%)
  other arithmetic  8.45 us (2%)
    reshape x8, local copies, waits for them, and re-layouts, toeplitz_taps(): tiled.reshape(filt_count, rows, span - 1)[:, :, rows - 1:rows - 1 + cols]  127 us
    all_gather x1, waiting for transfers between devices, local(): lax.all_gather(partial_out, 'chan')  56.7 us
    all_gather x2, waiting for transfers between devices, long_conv(): piece_field = lax.all_gather(field_cols, 'seq', axis=1, tiled=True)  46 us
    dot_general x8, matrix products, apply_taps(): jnp.einsum('gcs,gts->gct', grouped, taps, preferred_element_type=jnp.floa...  27.7 us
    while x40, local copies, waits for them, and re-layouts  23 us
    slice x8, local copies, waits for them, and re-layouts, toeplitz_taps(): tiled = jnp.tile(reversed_win, (1, rows))[:, :rows * (span - 1)]  17.9 us
    all_gather x1, blocking collectives, long_conv(): piece_segs = lax.all_gather(seg_row, 'seq', axis=1, tiled=True)  12.8 us
    dynamic_slice x8, local copies, waits for them, and re-layouts, one_block(): sub_field = lax.dynamic_slice_in_dim(piece_field, offset, tok_rows, 1)  7.8 us
  transfers between devices with their start and end apart: 3, of which 3 were waited for; matrix products, arithmetic and copies ran while one was open for 1% of the time, Pallas kernels for 0%

profile of v1, /device:TPU:0, one launch (start us, length us, event | category | flops | bytes accessed | tf_op | source)
XLA Modules:
  0.0 353.7 jit_solution(6705412265542900161)
XLA Ops:
  6.5 1.1 copy.15
  7.7 1.1 copy.16
  8.8 0.8 fusion.9
  9.7 1.1 copy.14
  10.8 12.8 %all-gather.2 = s32[4,1,128]{2,1,0:T(1,128)S(1)} all-gather(s32[1,1,128]{2,1,0:T(1,128)} %bitcast.66), channel_id=2, replica_groups=mesh['groups'=2,'seq'=4,'chan'=4] {'seq'}, dimensions={0}, use_global_device_ids=true | all-gather | bytes 2560 | tf_op jit(solution)/shard_map/all_gather | solution.py:44
  23.6 0.9 pad_maximum_fusion
  24.5 17.9 %all-gather.7.cloned.1.call-done = bf16[1024,512]{1,0:T(8,128)(2,1)} async-done(((bf16[1024,128]{1,0:T(8,128)(2,1)}), bf16[1024,512]{1,0:T(8,128)(2,1)}) %all-gather.7.cloned.1.call-update) | async-done | bytes 1048592 | tf_op jit(solution)/shard_map/all_gather | solution.py:43
  42.4 103.7 %while.36 = (s32[]{:T(128)}, f32[64,16,128]{2,1,0:T(8,128)S(1)}, bf16[1024,512]{1,0:T(8,128)(2,1)}, s32[]{:T(128)}, bf16[64,1024]{1,0:T(8,128)(2,1)S(1)}, /*inde...) while((s32[]{:T(128)}, f32[64,16,128]{2,1,0:T(8,128)S(1)}, ...), condition=%wide.region_1.2_spmd.clone, body=%wide.region_0.1_spmd.clone.sunk | while | flops 34897944 | bytes 33591060 | solution.py:58
  42.8 0.3 tile.60
  43.1 2.6 copy.21
  45.7 2.2 slice.78
  47.9 15.9 %reshape.159 = bf16[64,128,255]{2,1,0:T(8,128)(2,1)} reshape(bf16[64,32640]{1,0:T(8,128)(2,1)} %slice.78) | data formatting | bytes 8355840 | tf_op jit(solution)/shard_map/while/body/eval_jaxpr/reshape | solution.py:16
  63.9 1.0 constant_dynamic-slice_fusion.10
  64.9 3.5 fusion.23
  68.4 0.2 reverse.4
  68.7 0.3 tile.60
  69.0 2.6 copy.21
  71.6 2.2 slice.78
  73.9 15.9 %reshape.159 = bf16[64,128,255]{2,1,0:T(8,128)(2,1)} reshape(bf16[64,32640]{1,0:T(8,128)(2,1)} %slice.78) | data formatting | bytes 8355840 | tf_op jit(solution)/shard_map/while/body/eval_jaxpr/reshape | solution.py:16
  89.8 1.0 constant_dynamic-slice_fusion.10
  90.8 3.5 fusion.23
  94.7 0.3 tile.60
  94.9 2.6 copy.21
  97.6 2.2 slice.78
  99.8 15.9 %reshape.159 = bf16[64,128,255]{2,1,0:T(8,128)(2,1)} reshape(bf16[64,32640]{1,0:T(8,128)(2,1)} %slice.78) | data formatting | bytes 8355840 | tf_op jit(solution)/shard_map/while/body/eval_jaxpr/reshape | solution.py:16
  115.8 1.0 constant_dynamic-slice_fusion.10
  116.7 3.5 fusion.23
  120.6 0.3 tile.60
  120.9 2.6 copy.21
  123.5 2.2 slice.78
  125.7 15.9 %reshape.159 = bf16[64,128,255]{2,1,0:T(8,128)(2,1)} reshape(bf16[64,32640]{1,0:T(8,128)(2,1)} %slice.78) | data formatting | bytes 8355840 | tf_op jit(solution)/shard_map/while/body/eval_jaxpr/reshape | solution.py:16
  141.7 1.0 constant_dynamic-slice_fusion.10
  142.7 3.5 fusion.23
  146.1 0.8 fusion.8
  146.9 0.2 all-gather.11.cloned.1.call-start
  147.2 28.1 %all-gather.9.cloned.1.call-done = bf16[1024,512]{1,0:T(8,128)(2,1)} async-done(((bf16[1024,128]{1,0:T(8,128)(2,1)}), bf16[1024,512]{1,0:T(8,128)(2,1)}) %all-gather.9.cloned.1.call-update) | async-done | bytes 1048592 | tf_op jit(solution)/shard_map/all_gather | solution.py:43
  175.3 103.7 %while.37 = (s32[]{:T(128)}, f32[64,16,128]{2,1,0:T(8,128)S(1)}, bf16[1024,512]{1,0:T(8,128)(2,1)}, s32[]{:T(128)}, bf16[64,1024]{1,0:T(8,128)(2,1)S(1)}, /*inde...) while((s32[]{:T(128)}, f32[64,16,128]{2,1,0:T(8,128)S(1)}, ...), condition=%wide.region_3.4_spmd.clone, body=%wide.region_2.3_spmd.clone.sunk | while | flops 34897944 | bytes 33591060 | solution.py:58
  175.7 0.3 tile.61
  176.0 2.6 copy.22
  178.6 2.2 slice.81
  180.8 15.9 %reshape.160 = bf16[64,128,255]{2,1,0:T(8,128)(2,1)} reshape(bf16[64,32640]{1,0:T(8,128)(2,1)} %slice.81) | data formatting | bytes 8355840 | tf_op jit(solution)/shard_map/while/body/eval_jaxpr/reshape | solution.py:16
  196.8 1.0 constant_dynamic-slice_fusion.12
  197.8 3.5 fusion.26
  201.6 0.3 tile.61
  201.9 2.6 copy.22
  204.5 2.2 slice.81
  206.8 15.9 %reshape.160 = bf16[64,128,255]{2,1,0:T(8,128)(2,1)} reshape(bf16[64,32640]{1,0:T(8,128)(2,1)} %slice.81) | data formatting | bytes 8355840 | tf_op jit(solution)/shard_map/while/body/eval_jaxpr/reshape | solution.py:16
  222.7 1.0 constant_dynamic-slice_fusion.12
  223.7 3.5 fusion.26
  227.6 0.3 tile.61
  227.9 2.6 copy.22
  230.5 2.2 slice.81
  232.7 15.9 %reshape.160 = bf16[64,128,255]{2,1,0:T(8,128)(2,1)} reshape(bf16[64,32640]{1,0:T(8,128)(2,1)} %slice.81) | data formatting | bytes 8355840 | tf_op jit(solution)/shard_map/while/body/eval_jaxpr/reshape | solution.py:16
  248.7 1.0 constant_dynamic-slice_fusion.12
  249.7 3.5 fusion.26
  253.5 0.3 tile.61
  253.8 2.6 copy.22
  256.4 2.2 slice.81
  258.7 15.9 %reshape.160 = bf16[64,128,255]{2,1,0:T(8,128)(2,1)} reshape(bf16[64,32640]{1,0:T(8,128)(2,1)} %slice.81) | data formatting | bytes 8355840 | tf_op jit(solution)/shard_map/while/body/eval_jaxpr/reshape | solution.py:16
  274.6 1.0 constant_dynamic-slice_fusion.12
  275.6 3.5 fusion.26
  279.1 6.1 %fusion.10 = f32[128,4096]{1,0:T(8,128)} fusion(bf16[128,1024]{0,1:T(8,128)(2,1)S(1)} %bitcast.64, bf16[1024,4096]{1,0:T(8,128)(2,1)} %param.16), kind=kOutput, calls=%fused_computation.24 | convolution fusion | flops 1073741824 | bytes 10747904 | tf_op jit(solution)/shard_map/dot_general | solution.py:65
  285.2 56.7 %all-gather.11.cloned.1.call-done = f32[512,4096]{1,0:T(8,128)} async-done(((f32[128,4096]{1,0:T(8,128)}), f32[512,4096]{1,0:T(8,128)}) %all-gather.11.cloned.1.call-update) | async-done | bytes 8388624 | tf_op jit(solution)/shard_map/all_gather | solution.py:66
  341.9 5.3 %reduce_sum.9 = bf16[128,4096]{1,0:T(8,128)(2,1)} reduce(f32[4,128,4096]{2,1,0:T(8,128)} %bitcast.59, f32[]{:T(128)} %constant.222.clone.1), dimensions={0}, to_apply=%region_4.5 | reduce | flops 1572864 | bytes 9437188 | tf_op jit(solution)/shard_map/reduce_sum | solution.py:66
  (74 shorter events, 3.6 us)
Async XLA Ops:
  6.5 35.9 %all-gather.7.cloned.1.call-start = ((), (), s32[]{:S(2)}) async-start(), calls=%async_computation | async-start | bytes 1310720 | tf_op jit(solution)/shard_map/all_gather | solution.py:43
  9.6 165.7 %all-gather.9.cloned.1.call-start = ((), (), s32[]{:S(2)}) async-start(), calls=%async_computation.1 | async-start | bytes 1310720 | tf_op jit(solution)/shard_map/all_gather | solution.py:43
  42.4 104.8 %copy-start = (bf16[64,512]{1,0:T(8,128)(2,1)S(1)}, bf16[64,512]{1,0:T(8,128)(2,1)}, u32[]{:S(2)}) copy-start(bf16[64,512]{1,0:T(8,128)(2,1)} %param.15) | copy-start | bytes 196612
  47.9 15.9 %copy-start.1 = (s32[128]{0:T(128)S(1)}, s32[128]{0:T(128)}, u32[]{:S(2)}) copy-start(s32[128]{0:T(128)} %get-tuple-element.664) | copy-start | bytes 1540 | tf_op jit(solution)/shard_map/while
  73.9 15.9 %copy-start.1 = (s32[128]{0:T(128)S(1)}, s32[128]{0:T(128)}, u32[]{:S(2)}) copy-start(s32[128]{0:T(128)} %get-tuple-element.664) | copy-start | bytes 1540 | tf_op jit(solution)/shard_map/while
  99.8 15.9 %copy-start.1 = (s32[128]{0:T(128)S(1)}, s32[128]{0:T(128)}, u32[]{:S(2)}) copy-start(s32[128]{0:T(128)} %get-tuple-element.664) | copy-start | bytes 1540 | tf_op jit(solution)/shard_map/while
  125.7 15.9 %copy-start.1 = (s32[128]{0:T(128)S(1)}, s32[128]{0:T(128)}, u32[]{:S(2)}) copy-start(s32[128]{0:T(128)} %get-tuple-element.664) | copy-start | bytes 1540 | tf_op jit(solution)/shard_map/while
  146.9 195.0 %all-gather.11.cloned.1.call-start = ((), (), s32[]{:S(2)}) async-start(), calls=%async_computation.2 | async-start | bytes 10485760 | tf_op jit(solution)/shard_map/all_gather | solution.py:66
  180.8 15.9 %copy-start.2 = (s32[128]{0:T(128)S(1)}, s32[128]{0:T(128)}, u32[]{:S(2)}) copy-start(s32[128]{0:T(128)} %get-tuple-element.709) | copy-start | bytes 1540 | tf_op jit(solution)/shard_map/while
  206.8 15.9 %copy-start.2 = (s32[128]{0:T(128)S(1)}, s32[128]{0:T(128)}, u32[]{:S(2)}) copy-start(s32[128]{0:T(128)} %get-tuple-element.709) | copy-start | bytes 1540 | tf_op jit(solution)/shard_map/while
  232.7 15.9 %copy-start.2 = (s32[128]{0:T(128)S(1)}, s32[128]{0:T(128)}, u32[]{:S(2)}) copy-start(s32[128]{0:T(128)} %get-tuple-element.709) | copy-start | bytes 1540 | tf_op jit(solution)/shard_map/while
  258.7 15.9 %copy-start.2 = (s32[128]{0:T(128)S(1)}, s32[128]{0:T(128)}, u32[]{:S(2)}) copy-start(s32[128]{0:T(128)} %get-tuple-element.709) | copy-start | bytes 1540 | tf_op jit(solution)/shard_map/while
Sparse Core Ops, SparseCore 0:
  9.7 32.6 all-gather.6
  147.1 28.2 all-gather.8
  285.3 56.5 all-gather.10
